TPU v7x, 128 devices: a whole 4x4x4 slice. The times are simulated.
128 devices in a mesh: dp: 4 (over y_hi, core), mp: 32 (over x, z, y_lo).
Axes of the slice: x: 4, y: 4 (y_hi: 2, y_lo: 2; y = y_hi * 2 + y_lo), z: 4, core: 2. Of those that a mesh axis runs over, the one named last changes fastest.
Arguments:
- tokens: bfloat16 [8192, 3072], P(('dp', 'mp')), may hold values from -6 to 6
- cotangent: bfloat16 [8192, 3072], P(('dp', 'mp')), may hold values from -3 to 3
- w_qkv: bfloat16 [3072, 32, 384], P(None, 'mp'), may hold values from -0.109375 to 0.109375
- w_out: bfloat16 [32, 128, 3072], P('mp'), may hold values from -0.09375 to 0.09375
- moment_qkv: float32 [3072, 32, 384], P('dp', 'mp'), may hold values from -6 to 6
- second_qkv: float32 [3072, 32, 384], P('dp', 'mp'), may hold values from 0.01 to 100
- moment_out: float32 [32, 128, 3072], P('mp', None, 'dp'), may hold values from -6 to 6
- second_out: float32 [32, 128, 3072], P('mp', None, 'dp'), may hold values from 0.01 to 100
Outputs:
- input_grad: bfloat16 [8192, 3072], P(('dp', 'mp'))
- new_moment_qkv: float32 [3072, 32, 384], P('dp', 'mp')
- new_second_qkv: float32 [3072, 32, 384], P('dp', 'mp')
- update_qkv: float32 [3072, 32, 384], P('dp', 'mp')
- new_moment_out: float32 [32, 128, 3072], P('mp', None, 'dp')
- new_second_out: float32 [32, 128, 3072], P('mp', None, 'dp')
- update_out: float32 [32, 128, 3072], P('mp', None, 'dp')
All inputs are finite; a program needn't handle non-finite values.
Results may differ from a plain program's by a relative error of at most 0.035.
Values may be sent and summed in bfloat16 or wider, within the bound.
No kernel may reach another device: no remote copies, remote signals or barrier semaphores. Data moves between devices by JAX's collectives and lax.ppermute only.
A program may use at most 128 MiB of HBM per device.

v0:
```python
from functools import partial
import math
import jax
import jax.numpy as jnp
from jax import lax
from jax.sharding import PartitionSpec as P

SEQ = 256
beta_one = 0.9
beta_two = 0.95
step_count = 10
eps_base = 0.001
norm_eps = 1e-06


def normalize(block):
    centre = block - jnp.mean(block, axis=-1, keepdims=True)
    return centre / jnp.sqrt(jnp.mean(centre * centre, axis=-1, keepdims=True) + norm_eps)


def attend(packed, seq):
    head_width = packed.shape[1] // 3
    blocks = packed.reshape(packed.shape[0] // seq, seq, 3 * head_width)
    query_rows = normalize(blocks[:, :, :head_width])
    key_matrix_rows = normalize(blocks[:, :, head_width : 2 * head_width])
    value_matrix_rows = blocks[:, :, 2 * head_width :]
    attention_scores = jnp.einsum("oaw,ozw->oaz", query_rows, key_matrix_rows) / math.sqrt(
        head_width
    )
    attention_weights = jnp.exp(attention_scores)
    attention_weights = attention_weights / jnp.sum(attention_weights, axis=-1, keepdims=True)
    mixed_heads_output = jnp.einsum("ryn,rni->ryi", attention_weights, value_matrix_rows)
    return mixed_heads_output.reshape(packed.shape[0], head_width)


def adam_step(grad, moment, second, fan_in):
    new_moment = beta_one * moment + (1.0 - beta_one) * grad
    new_second = beta_two * second + (1.0 - beta_two) * grad * grad
    corrected = new_moment / (1.0 - beta_one**step_count)
    scaled = new_second / (1.0 - beta_two**step_count)
    update = -corrected / (jnp.sqrt(scaled) + eps_base / math.sqrt(fan_in))
    return (new_moment, new_second, update)


def shards(tokens, cotangent, w_qkv, w_out, moment_qkv, second_qkv, moment_out, second_out):
    rows = lax.all_gather(tokens, "mp", axis=0, tiled=True)
    cot_rows = lax.all_gather(cotangent, "mp", axis=0, tiled=True)
    projection = w_qkv[:, 0, :]
    out_rows = w_out[0]
    packed = jnp.dot(rows, projection, preferred_element_type=jnp.float32).astype(jnp.bfloat16)
    mixed_heads_output, backward = jax.vjp(partial(attend, seq=SEQ), packed.astype(jnp.float32))
    mixed_low = mixed_heads_output.astype(jnp.bfloat16)
    dmix = jnp.dot(cot_rows, out_rows.T, preferred_element_type=jnp.float32).astype(jnp.bfloat16)
    out_part = jnp.dot(mixed_low.T, cot_rows, preferred_element_type=jnp.float32)
    packed_grad = backward(dmix.astype(jnp.float32))[0].astype(jnp.bfloat16)
    qkv_part = jnp.dot(rows.T, packed_grad, preferred_element_type=jnp.float32)
    whole_term = jnp.dot(packed_grad, projection.T, preferred_element_type=jnp.float32)
    input_grad = lax.psum_scatter(
        whole_term.astype(jnp.bfloat16), "mp", scatter_dimension=0, tiled=True
    )
    summed_qkv, summed_out = (
        lax.psum_scatter(
            qkv_part[:, None, :].astype(jnp.bfloat16), "dp", scatter_dimension=0, tiled=True
        ).astype(jnp.float32),
        lax.psum_scatter(
            out_part[None].astype(jnp.bfloat16), "dp", scatter_dimension=2, tiled=True
        ).astype(jnp.float32),
    )
    width_in = w_qkv.shape[0]
    heads_width = w_out.shape[0] * w_out.shape[1] * lax.axis_size("mp")
    m_qkv, s_qkv, u_qkv = adam_step(summed_qkv, moment_qkv, second_qkv, width_in)
    m_out, s_out, u_out = adam_step(summed_out, moment_out, second_out, heads_width)
    return (input_grad, m_qkv, s_qkv, u_qkv, m_out, s_out, u_out)


def solution(mesh):
    placed = (
        P(("dp", "mp"), None),
        P(("dp", "mp"), None),
        P(None, "mp", None),
        P("mp", None, None),
        P("dp", "mp", None),
        P("dp", "mp", None),
        P("mp", None, "dp"),
        P("mp", None, "dp"),
    )
    return jax.shard_map(
        shards,
        mesh=mesh,
        in_specs=placed,
        out_specs=(
            P(("dp", "mp"), None),
            P("dp", "mp", None),
            P("dp", "mp", None),
            P("dp", "mp", None),
            P("mp", None, "dp"),
            P("mp", None, "dp"),
            P("mp", None, "dp"),
        ),
        check_vma=False,
    )
```

profile of v0, /device:TPU:0, one launch (start us, length us, event | category | flops | bytes accessed | tf_op | source)
XLA Modules:
  0.0 927.5 jit_solution(5022044100297365708)
XLA Ops:
  8.7 277.4 %all-gather.3.cloned.1.call-done = bf16[2048,3072]{1,0:T(8,128)(2,1)} async-done(((bf16[64,3072]{1,0:T(8,128)(2,1)}), bf16[2048,3072]{1,0:T(8,128)(2,1)}) %all-gather.3.cloned.1.call-update) | async-done | bytes 12582928 | tf_op jit(solution)/shard_map/all_gather | solution.py:46
  286.1 9.6 %bitcast_convert_fusion = (f32[8,256,384]{2,1,0:T(8,128)S(1)}, bf16[2048,384]{1,0:T(8,128)(2,1)S(1)}) fusion(bf16[2048,3072]{1,0:T(8,128)(2,1)} %all-gather.3.cloned.1.call-done, bf16[3072,1,384]{2,0,1:T(8,128)(2,1)S(1)} %copy-done), kind=kOutput, calls=%fused_computation.59 | convolution fusion | flops 4833411072 | bytes 19660800 | tf_op jit(solution)/shard_map/dot_general | solution.py:50
  296.3 1.3 multiply_reduce_fusion.4
  297.7 2.8 fusion.29
  300.6 1.4 copy-done.4
  302.5 260.6 %all-gather.5.cloned.1.call-done = bf16[2048,3072]{1,0:T(8,128)(2,1)} async-done(((bf16[64,3072]{1,0:T(8,128)(2,1)}), bf16[2048,3072]{1,0:T(8,128)(2,1)}) %all-gather.5.cloned.1.call-update) | async-done | bytes 12582928 | tf_op jit(solution)/shard_map/all_gather | solution.py:47
  563.0 7.3 fusion.1
  570.6 8.3 convolution_convert_fusion.4
  578.9 1.7 multiply_reduce_fusion
  581.1 3.1 multiply_reduce_fusion.2
  584.2 4.0 fusion.23
  588.2 1.3 fusion.24
  589.5 2.6 broadcast_add_fusion.1
  593.9 6.4 fusion
  600.6 11.2 %convolution_convert_fusion = bf16[2048,3072]{1,0:T(8,128)(2,1)} fusion(bf16[2048,384]{1,0:T(8,128)(2,1)} %bitcast.31, bf16[3072,1,384]{2,0,1:T(8,128)(2,1)S(1)} %copy-done), kind=kOutput, calls=%fused_computation | convolution fusion | flops 4838129664 | bytes 16515072 | tf_op jit(solution)/shard_map/dot_general | solution.py:57
  611.8 3.4 copy.16
  615.3 4.7 copy.17
  620.0 2.4 add_divide_fusion.1
  622.3 21.8 %reduce-scatter.6.cloned.1.call-done = bf16[768,1,384]{0,2,1:T(8,128)(2,1)} async-done(((bf16[3072,1,384]{0,2,1:T(8,128)(2,1)}), bf16[768,1,384]{0,2,1:T(8,128)(2,1)}) %reduce-scatter.6.cloned.1.call-update) | async-done | bytes 589840 | tf_op jit(solution)/shard_map/reduce_scatter | solution.py:62
  644.2 3.7 add_divide_fusion
  647.8 4.8 copy.21
  652.6 4.7 copy.20
  657.3 2.6 copy.19
  660.0 261.0 %reduce-scatter.4.cloned.1.call-done = bf16[64,3072]{1,0:T(8,128)(2,1)} async-done(((bf16[2048,3072]{1,0:T(8,128)(2,1)}), bf16[64,3072]{1,0:T(8,128)(2,1)}) %reduce-scatter.4.cloned.1.call-update) | async-done | bytes 393232 | tf_op jit(solution)/shard_map/reduce_scatter | solution.py:58
  (46 shorter events, 5.5 us)
Async XLA Ops:
  7.2 278.9 %copy-start = (bf16[3072,1,384]{2,0,1:T(8,128)(2,1)S(1)}, bf16[3072,1,384]{2,0,1:T(8,128)(2,1)}, u32[]{:S(2)}) copy-start(bf16[3072,1,384]{2,0,1:T(8,128)(2,1)} %param.10) | copy-start | bytes 7077892
  7.2 278.9 %all-gather.3.cloned.1.call-start = ((), (), s32[]{:S(2)}) async-start(), calls=%async_computation.3 | async-start | bytes 12976128 | tf_op jit(solution)/shard_map/all_gather | solution.py:46
  7.9 555.1 %all-gather.5.cloned.1.call-start = ((), (), s32[]{:S(2)}) async-start(), calls=%async_computation.4 | async-start | bytes 12976128 | tf_op jit(solution)/shard_map/all_gather | solution.py:47
  8.7 611.3 %reduce-scatter.8.cloned.1.call-start = ((), (), s32[]{:S(2)}) async-start(), calls=%async_computation.7 | async-start | bytes 983040 | tf_op jit(solution)/shard_map/reduce_scatter | solution.py:65
  295.7 2.0 copy-start.1
  295.7 4.8 copy-start.7
  300.5 1.4 copy-start.4
  570.3 73.8 %reduce-scatter.6.cloned.1.call-start = ((), (), s32[]{:S(2)}) async-start(), calls=%async_computation.6 | async-start | bytes 2949120 | tf_op jit(solution)/shard_map/reduce_scatter | solution.py:62
  570.6 8.3 copy-start.5
  578.9 2.2 copy-start.2
  584.2 9.7 %slice-start = ((s8[12582912]{0:T(1024)(128)(4,1)}), s8[4194304]{0:T(1024)(128)(4,1)S(1)}, s32[]{:S(2)}) async-start(s8[12582912]{0:T(1024)(128)(4,1)} %bitcast.37), calls=%async_computation.8 | async-start | bytes 8388608
  584.2 9.7 %slice-start.1 = ((s8[12582912]{0:T(1024)(128)(4,1)}), s8[4194304]{0:T(1024)(128)(4,1)S(1)}, s32[]{:S(2)}) async-start(s8[12582912]{0:T(1024)(128)(4,1)} %bitcast.37), calls=%async_computation.9 | async-start | bytes 8388608
  589.5 4.4 slice-start.2
  592.7 1.2 copy-start.6
  600.4 320.6 %reduce-scatter.4.cloned.1.call-start = ((), (), s32[]{:S(2)}) async-start(), calls=%async_computation.5 | async-start | bytes 12976128 | tf_op jit(solution)/shard_map/reduce_scatter | solution.py:58
  647.8 9.5 %copy-start.3 = (f32[768,1,384]{0,2,1:T(8,128)S(1)}, f32[768,1,384]{0,2,1:T(8,128)}, u32[]{:S(2)}) copy-start(f32[768,1,384]{0,2,1:T(8,128)} %get-tuple-element.25) | copy-start | bytes 3538948
Sparse Core Ops, SparseCore 0:
  9.7 276.3 all-gather.2
  287.7 275.2 all-gather.4
  570.4 31.5 reduce-scatter.7
  604.8 39.3 reduce-scatter.5
  647.0 273.9 reduce-scatter.3
where the time goes:
time: 928 us
  waiting for transfers between devices  822 us (89%)
  matrix products  55.3 us (6%)
  local copies, waits for them, and re-layouts  23.3 us (3%)
  between operations  14.1 us (2%)
  other arithmetic  12 us (1%)
    all_gather x1, waiting for transfers between devices, shards(): rows = lax.all_gather(tokens, 'mp', axis=0, tiled=True)  277 us
    reduce_scatter x1, waiting for transfers between devices, shards(): lax.psum_scatter(whole_term.astype(jnp.bfloat16), 'mp', scatter_dimension...  261 us
    all_gather x1, waiting for transfers between devices, shards(): cot_rows = lax.all_gather(cotangent, 'mp', axis=0, tiled=True)  261 us
    unnamed x27, local copies, waits for them, and re-layouts  23.3 us
    reduce_scatter x1, waiting for transfers between devices, shards(): lax.psum_scatter(qkv_part[:, None, :].astype(jnp.bfloat16), 'dp', scatter...  21.8 us
  transfers between devices with their start and end apart: 5, of which 4 were waited for; matrix products, arithmetic and copies ran while one was open for 9% of the time, Pallas kernels for 0%

commit v1 on v0

--- a/solution.py
+++ b/solution.py
@@ -43,7 +43,9 @@
 
 
 def shards(tokens, cotangent, w_qkv, w_out, moment_qkv, second_qkv, moment_out, second_out):
-    rows = lax.all_gather(tokens, "mp", axis=0, tiled=True)
+    rows = jnp.concatenate(
+        lax.all_to_all(jnp.stack([tokens] * lax.axis_size("mp")), "mp", 0, 0), axis=0
+    )
     cot_rows = lax.all_gather(cotangent, "mp", axis=0, tiled=True)
     projection = w_qkv[:, 0, :]
     out_rows = w_out[0]

time: 928 us -> 790 us (0.85)
  waiting for transfers between devices: 822 us -> 481 us
  blocking collectives: 0 us -> 198 us
    all_gather x1 -> x0, waiting for transfers between devices: 277 us -> none  [shards(): rows = lax.all_gather(tokens, 'mp', axis=0, tiled=True)]
    all_to_all x0 -> x1, blocking collectives: none -> 198 us  [shards(): lax.all_to_all(jnp.stack([tokens] * lax.axis_size('mp')), 'mp', 0, 0)]
    all_gather x1, waiting for transfers between devices: 261 us -> 194 us  [shards(): cot_rows = lax.all_gather(cotangent, 'mp', axis=0, tiled=True)]
    unnamed x27 -> x29, local copies, waits for them, and re-layouts: 23.3 us -> 23.2 us
  transfers between devices with their start and end apart: 5 -> 4, of which waited for: 4 -> 3; matrix products, arithmetic and copies ran while one was open for 9% -> 11% of each run, Pallas kernels for 0% -> 0%
where the time goes in v1:
time: 790 us; the launch traced here: 789 us
  waiting for transfers between devices  481 us (61%)
  blocking collectives  198 us (25%)
  matrix products  52.5 us (7%)
  local copies, waits for them, and re-layouts  30.4 us (4%)
  between operations  14.1 us (2%)
  other arithmetic  12.1 us (2%)
    reduce_scatter x1, waiting for transfers between devices, shards(): lax.psum_scatter(whole_term.astype(jnp.bfloat16), 'mp', scatter_dimension...  261 us
    all_to_all x1, blocking collectives, shards(): lax.all_to_all(jnp.stack([tokens] * lax.axis_size('mp')), 'mp', 0, 0)  198 us
    all_gather x1, waiting for transfers between devices, shards(): cot_rows = lax.all_gather(cotangent, 'mp', axis=0, tiled=True)  194 us
    reduce_scatter x1, waiting for transfers between devices, shards(): lax.psum_scatter(qkv_part[:, None, :].astype(jnp.bfloat16), 'dp', scatter...  25.2 us
    unnamed x29, local copies, waits for them, and re-layouts  23.2 us
  transfers between devices with their start and end apart: 4, of which 3 were waited for; matrix products, arithmetic and copies ran while one was open for 11% of the time, Pallas kernels for 0%

profile of v1, /device:TPU:0, one launch (start us, length us, event | category | flops | bytes accessed | tf_op | source)
XLA Modules:
  0.0 789.0 jit_solution(6619462740013482106)
XLA Ops:
  8.0 7.2 stack.2
  15.1 198.0 %all_to_all.5 = bf16[32,64,3072]{2,1,0:T(8,128)(2,1)S(1)} all-to-all(bf16[32,64,3072]{2,1,0:T(8,128)(2,1)} %stack.2), channel_id=1, replica_groups=mesh['dp'=4,'mp'=32] {'mp'}, dimensions={0} | all-to-all | bytes 25165824 | tf_op jit(solution)/shard_map/all_to_all | solution.py:47
  213.1 6.7 bitcast_convert_fusion
  221.9 2.8 fusion.29
  224.8 1.4 copy-done.5
  226.7 194.5 %all-gather.2.cloned.1.call-done = bf16[2048,3072]{1,0:T(8,128)(2,1)} async-done(((bf16[64,3072]{1,0:T(8,128)(2,1)}), bf16[2048,3072]{1,0:T(8,128)(2,1)}) %all-gather.2.cloned.1.call-update) | async-done | bytes 12582928 | tf_op jit(solution)/shard_map/all_gather | solution.py:49
  421.1 7.3 fusion.1
  428.7 8.3 %convolution_convert_fusion.4 = bf16[2048,128]{1,0:T(8,128)(2,1)S(1)} fusion(bf16[2048,3072]{1,0:T(8,128)(2,1)} %all-gather.2.cloned.1.call-done, bf16[1,128,3072]{2,1,0:T(8,128)(2,1)} %param.11), kind=kOutput, calls=%fused_computation.7 | convolution fusion | flops 1610874880 | bytes 13893632 | tf_op jit(solution)/shard_map/dot_general | solution.py:55
  437.0 1.6 multiply_reduce_fusion
  439.0 3.1 multiply_reduce_fusion.2
  442.2 4.0 fusion.23
  446.2 1.3 fusion.24
  447.5 2.6 broadcast_add_fusion.1
  451.9 6.4 fusion
  458.6 11.2 %convolution_convert_fusion = bf16[2048,3072]{1,0:T(8,128)(2,1)} fusion(bf16[2048,384]{1,0:T(8,128)(2,1)} %bitcast.36, bf16[3072,1,384]{2,0,1:T(8,128)(2,1)S(1)} %copy-done), kind=kOutput, calls=%fused_computation | convolution fusion | flops 4838129664 | bytes 16515072 | tf_op jit(solution)/shard_map/dot_general | solution.py:59
  469.9 3.4 copy.16
  473.3 4.8 copy.17
  478.1 2.4 add_divide_fusion.1
  480.4 25.2 %reduce-scatter.6.cloned.1.call-done = bf16[768,1,384]{0,2,1:T(8,128)(2,1)} async-done(((bf16[3072,1,384]{0,2,1:T(8,128)(2,1)}), bf16[768,1,384]{0,2,1:T(8,128)(2,1)}) %reduce-scatter.6.cloned.1.call-update) | async-done | bytes 589840 | tf_op jit(solution)/shard_map/reduce_scatter | solution.py:64
  505.6 3.7 add_divide_fusion
  509.3 4.8 copy.19
  514.0 4.7 copy.20
  518.8 2.6 copy.21
  521.4 261.0 %reduce-scatter.4.cloned.1.call-done = bf16[64,3072]{1,0:T(8,128)(2,1)} async-done(((bf16[2048,3072]{1,0:T(8,128)(2,1)}), bf16[64,3072]{1,0:T(8,128)(2,1)}) %reduce-scatter.4.cloned.1.call-update) | async-done | bytes 393232 | tf_op jit(solution)/shard_map/reduce_scatter | solution.py:60
  (47 shorter events, 6.0 us)
Async XLA Ops:
  7.2 206.0 %copy-start = (bf16[3072,1,384]{2,0,1:T(8,128)(2,1)S(1)}, bf16[3072,1,384]{2,0,1:T(8,128)(2,1)}, u32[]{:S(2)}) copy-start(bf16[3072,1,384]{2,0,1:T(8,128)(2,1)} %param.10) | copy-start | bytes 7077892
  7.2 413.9 %all-gather.2.cloned.1.call-start = ((), (), s32[]{:S(2)}) async-start(), calls=%async_computation.4 | async-start | bytes 12976128 | tf_op jit(solution)/shard_map/all_gather | solution.py:49
  7.9 470.1 %reduce-scatter.8.cloned.1.call-start = ((), (), s32[]{:S(2)}) async-start(), calls=%async_computation.7 | async-start | bytes 983040 | tf_op jit(solution)/shard_map/reduce_scatter | solution.py:67
  213.1 6.7 copy-start.3
  219.9 2.0 copy-start.1
  219.9 4.8 copy-start.8
  224.7 1.4 copy-start.5
  428.4 77.2 %reduce-scatter.6.cloned.1.call-start = ((), (), s32[]{:S(2)}) async-start(), calls=%async_computation.6 | async-start | bytes 2949120 | tf_op jit(solution)/shard_map/reduce_scatter | solution.py:64
  428.6 8.3 %copy-start.6 = (f32[8,256,256]{1,2,0:T(8,128)S(1)}, f32[8,256,256]{1,2,0:T(8,128)}, u32[]{:S(2)}) copy-start(f32[8,256,256]{1,2,0:T(8,128)} %copy-done.5) | copy-start | bytes 6291460
  437.0 2.0 copy-start.2
  442.1 9.8 %slice-start = ((s8[12582912]{0:T(1024)(128)(4,1)}), s8[4194304]{0:T(1024)(128)(4,1)S(1)}, s32[]{:S(2)}) async-start(s8[12582912]{0:T(1024)(128)(4,1)} %bitcast.32), calls=%async_computation.8 | async-start | bytes 8388608
  442.1 9.7 %slice-start.1 = ((s8[12582912]{0:T(1024)(128)(4,1)}), s8[4194304]{0:T(1024)(128)(4,1)S(1)}, s32[]{:S(2)}) async-start(s8[12582912]{0:T(1024)(128)(4,1)} %bitcast.32), calls=%async_computation.9 | async-start | bytes 8388608
  447.5 4.4 slice-start.2
  450.7 1.2 copy-start.7
  458.4 324.1 %reduce-scatter.4.cloned.1.call-start = ((), (), s32[]{:S(2)}) async-start(), calls=%async_computation.5 | async-start | bytes 12976128 | tf_op jit(solution)/shard_map/reduce_scatter | solution.py:60
  509.3 9.5 %copy-start.4 = (f32[768,1,384]{0,2,1:T(8,128)S(1)}, f32[768,1,384]{0,2,1:T(8,128)}, u32[]{:S(2)}) copy-start(f32[768,1,384]{0,2,1:T(8,128)} %get-tuple-element.23) | copy-start | bytes 3538948
Sparse Core Ops, SparseCore 0:
  9.7 411.3 all-gather.1
  428.5 34.8 reduce-scatter.7
  466.2 39.3 reduce-scatter.5
  508.5 273.9 reduce-scatter.3
